TPU v7x, 256 devices: a whole 4x4x8 slice. The times are simulated.
256 devices in a mesh: wide: 32 (over y, x, core), narrow: 8 (over z).
Axes of the slice: x: 4, y: 4, z: 8, core: 2. Of those that a mesh axis runs over, the one named last changes fastest.
Arguments:
- up_grads: float32 [32, 192, 11008], P('wide', 'narrow'), may hold values from -6 to 6, as said below
- down_grads: float32 [32, 512, 4096], P('wide', 'narrow'), may hold values from -6 to 6, as said below
- gain_grads: float32 [32, 4096], P('wide', 'narrow'), may hold values from -6 to 6
- up_master: float32 [192, 11008], P('narrow', 'wide'), may hold values from -60 to 60, as said below
- down_master: float32 [512, 4096], P('narrow', 'wide'), may hold values from -60 to 60, as said below
- gain_master: float32 [4096], P(('narrow', 'wide')), may hold values from 0.5 to 1.5
- up_first: float32 [192, 11008], P('narrow', 'wide'), may hold values from -1.8 to 1.8, as said below
- down_first: float32 [512, 4096], P('narrow', 'wide'), may hold values from -1.8 to 1.8, as said below
- gain_first: float32 [4096], P(('narrow', 'wide')), may hold values from -4 to 4
- up_second: float32 [192, 11008], P('narrow', 'wide'), may hold values from 0.01 to 1
- down_second: float32 [512, 4096], P('narrow', 'wide'), may hold values from 0.01 to 1
- gain_second: float32 [4096], P(('narrow', 'wide')), may hold values from 0.01 to 1
Outputs:
- up_first_new: float32 [192, 11008], P('narrow', 'wide')
- up_second_new: float32 [192, 11008], P('narrow', 'wide')
- up_master_new: float32 [192, 11008], P('narrow', 'wide')
- up_weights: bfloat16 [192, 11008], replicated
- down_first_new: float32 [512, 4096], P('narrow', 'wide')
- down_second_new: float32 [512, 4096], P('narrow', 'wide')
- down_master_new: float32 [512, 4096], P('narrow', 'wide')
- down_weights: bfloat16 [512, 4096], replicated
- gain_first_new: float32 [4096], P(('narrow', 'wide'))
- gain_second_new: float32 [4096], P(('narrow', 'wide'))
- gain_master_new: float32 [4096], P(('narrow', 'wide'))
- gain_weights: bfloat16 [4096], replicated
Inputs may be any that keep to these rules, and one draw needn't show every extreme that they name: `up_master`: finite real entries. `down_master`: finite real entries. `up_grads`: finite real entries. `down_grads`: finite real entries. `up_first`: finite real entries. `down_first`: finite real entries.
All inputs are finite; a program needn't handle non-finite values.
Results may differ from a plain program's by a relative error of at most 0.001.
Values may be sent and summed in bfloat16 or wider, within the bound.
No kernel may reach another device: no remote copies, remote signals or barrier semaphores. Data moves between devices by JAX's collectives and lax.ppermute only.
A program may use at most 64 MiB of HBM per device.

v0:
```python
import jax
import jax.numpy as jnp
from jax import lax
from jax.sharding import PartitionSpec as P

BETA_ONE = 0.9
BETA_TWO = 0.999
EPSILON = 1e-06
LEARN_RATE = 0.05
DECAY_RATE = 0.01
CORRECT_FIRST = 1.0 - 0.9**10
CORRECT_SECOND = 1.0 - 0.999**10
LANES = 128


def moments(grad_sum, master, first, second, decay):
    first_new = BETA_ONE * first + (1.0 - BETA_ONE) * grad_sum
    second_new = BETA_TWO * second + (1.0 - BETA_TWO) * grad_sum * grad_sum
    update = (
        first_new / CORRECT_FIRST / (jnp.sqrt(second_new / CORRECT_SECOND) + EPSILON)
        + decay * master
    )
    return (first_new, second_new, update)


def finish(master, update, weight_sq, update_sq):
    trust = jnp.sqrt(weight_sq) / (jnp.sqrt(update_sq) + EPSILON)
    return master - LEARN_RATE * trust * update


def padded(total):
    return -(-total // LANES) * LANES


def body(
    up_grads,
    down_grads,
    gain_grads,
    up_master,
    down_master,
    gain_master,
    up_first,
    down_first,
    gain_first,
    up_second,
    down_second,
    gain_second,
):
    n_wide = lax.axis_size("wide")
    n_narrow = lax.axis_size("narrow")
    up_rows, up_cols = up_master.shape
    down_rows, down_cols = down_master.shape
    gain_cols = gain_master.shape[0]
    up_size = up_rows * up_cols
    down_size = down_rows * down_cols
    total = up_size + down_size + gain_cols
    width = padded(total)
    weight_sums = (
        jnp.sum(up_master * up_master),
        jnp.sum(down_master * down_master),
        jnp.sum(gain_master * gain_master),
    )
    up_part = up_grads[0].reshape(up_rows, n_wide, up_cols).transpose(1, 0, 2)
    down_part = down_grads[0].reshape(down_rows, n_wide, down_cols).transpose(1, 0, 2)
    gain_part = gain_grads.reshape(n_wide, gain_cols)
    packed = jnp.concatenate(
        [
            up_part.reshape(n_wide, up_size),
            down_part.reshape(n_wide, down_size),
            gain_part,
            jnp.zeros((n_wide, width - total), jnp.float32),
        ],
        axis=1,
    ).reshape(n_wide, width // LANES, LANES)
    summed = lax.psum_scatter(packed, "wide", scatter_dimension=0, tiled=True)
    summed = summed.reshape(width)
    up_sum = summed[:up_size].reshape(up_rows, up_cols)
    down_sum = summed[up_size : up_size + down_size].reshape(down_rows, down_cols)
    gain_sum = summed[up_size + down_size : total]
    up_first_new, up_second_new, up_update = moments(
        up_sum, up_master, up_first, up_second, DECAY_RATE
    )
    down_first_new, down_second_new, down_update = moments(
        down_sum, down_master, down_first, down_second, DECAY_RATE
    )
    gain_first_new, gain_second_new, gain_update = moments(
        gain_sum, gain_master, gain_first, gain_second, 0.0
    )
    weight_sums, update_sums = lax.psum(
        (
            weight_sums,
            (
                jnp.sum(up_update * up_update),
                jnp.sum(down_update * down_update),
                jnp.sum(gain_update * gain_update),
            ),
        ),
        ("wide", "narrow"),
    )
    up_master_new = finish(up_master, up_update, weight_sums[0], update_sums[0])
    down_master_new = finish(down_master, down_update, weight_sums[1], update_sums[1])
    gain_master_new = finish(gain_master, gain_update, weight_sums[2], update_sums[2])
    low = jnp.concatenate(
        [
            up_master_new.astype(jnp.bfloat16).reshape(up_size),
            down_master_new.astype(jnp.bfloat16).reshape(down_size),
            gain_master_new.astype(jnp.bfloat16),
            jnp.zeros((width - total,), jnp.bfloat16),
        ]
    ).reshape(1, width // LANES, LANES)
    whole = lax.all_gather(low, ("narrow", "wide"), axis=0, tiled=True)
    whole = whole.reshape(n_narrow, n_wide, width)
    up_weights = (
        whole[:, :, :up_size]
        .reshape(n_narrow, n_wide, up_rows, up_cols)
        .transpose(0, 2, 1, 3)
        .reshape(n_narrow * up_rows, n_wide * up_cols)
    )
    down_weights = (
        whole[:, :, up_size : up_size + down_size]
        .reshape(n_narrow, n_wide, down_rows, down_cols)
        .transpose(0, 2, 1, 3)
        .reshape(n_narrow * down_rows, n_wide * down_cols)
    )
    gain_weights = whole[:, :, up_size + down_size : total].reshape(-1)
    return (
        up_first_new,
        up_second_new,
        up_master_new,
        up_weights,
        down_first_new,
        down_second_new,
        down_master_new,
        down_weights,
        gain_first_new,
        gain_second_new,
        gain_master_new,
        gain_weights,
    )


def solution(mesh):
    return jax.shard_map(
        body,
        mesh=mesh,
        in_specs=(
            P("wide", "narrow", None),
            P("wide", "narrow", None),
            P("wide", "narrow"),
            P("narrow", "wide"),
            P("narrow", "wide"),
            P(("narrow", "wide")),
            P("narrow", "wide"),
            P("narrow", "wide"),
            P(("narrow", "wide")),
            P("narrow", "wide"),
            P("narrow", "wide"),
            P(("narrow", "wide")),
        ),
        out_specs=(
            P("narrow", "wide"),
            P("narrow", "wide"),
            P("narrow", "wide"),
            P(),
            P("narrow", "wide"),
            P("narrow", "wide"),
            P("narrow", "wide"),
            P(),
            P(("narrow", "wide")),
            P(("narrow", "wide")),
            P(("narrow", "wide")),
            P(),
        ),
        check_vma=False,
    )
```

profile of v0, /device:TPU:1, one launch (start us, length us, event | category | flops | bytes accessed | tf_op | source)
XLA Modules:
  0.0 378.5 jit_solution(11554978971868273810)
XLA Ops:
  7.2 0.0 copy-start.1
  7.2 0.0 reduce-scatter.4.cloned.1.call-start
  7.2 0.5 broadcast.49
  7.7 1.3 reduce.3
  9.1 0.1 reshape.74
  9.2 1.4 copy.34
  10.6 0.6 copy.31
  11.2 1.6 copy.43
  12.8 0.0 copy-done.1
  12.8 1.3 reshape_squeeze.6
  14.1 0.7 copy.42
  14.8 0.3 reshape.72
  15.1 2.5 concatenate.6
  17.7 0.0 copy-start.12
  17.7 0.0 copy-start.13
  17.7 0.0 copy-start.14
  17.7 0.0 copy-start.5
  17.7 0.0 copy-start.10
  17.7 0.0 copy-start.11
  17.7 0.0 copy-start.2
  17.8 0.0 copy-start.8
  17.8 0.0 copy-start.9
  17.8 1.5 reshape.75
  19.3 0.0 reduce-scatter.4.cloned.1.call-update
  19.3 0.0 all-gather.2.cloned.1.call-start
  19.4 85.1 %reduce-scatter.4.cloned.1.call-done = f32[1,129,128]{2,1,0:T(8,128)} async-done(((f32[32,129,128]{2,1,0:T(8,128)}), f32[1,129,128]{2,1,0:T(8,128)}) %reduce-scatter.4.cloned.1.call-update) | async-done | bytes 66064
  104.5 0.0 copy-done.12
  104.5 0.0 copy-done.13
  104.5 0.0 copy-done.14
  104.5 1.9 multiply_reduce_fusion.4
  106.3 0.0 copy-done.5
  106.3 0.0 copy-done.10
  106.3 0.0 copy-done.11
  106.3 1.5 multiply_reduce_fusion.2
  107.8 1.0 slice.21
  108.9 0.0 copy-done.2
  108.9 0.0 copy-done.8
  108.9 0.0 copy-done.9
  108.9 0.7 multiply_reduce_fusion
  109.5 78.0 %all-reduce.1 = (f32[]{:T(128)}, f32[]{:T(128)}, f32[]{:T(128)}, f32[]{:T(128)}, f32[]{:T(128)}, /*index=5*/f32[]{:T(128)}) all-reduce(f32[]{:T(128)} %get-tuple-element.13, f32[]{:T(128)} %get-tuple-element.12, f32[]{:T(128)} %get-tuple-element.15, f32[]{:T(128)} %get-tuple-element.14, ...), channel_id=1, replica_groups=mesh['wide'=32,'narrow'=8] {'wide','narrow'}, use_global_device_ids=true, to_apply=%region_2.0 | all-reduce | flops 6 | bytes 48 | tf_op jit(solution)/shard_map/psum | solution.py:89
  191.8 0.6 fusion.4
  192.5 0.1 reshape.76
  192.6 0.5 fusion.3
  193.1 0.6 convert_bitcast_fusion
  193.7 0.7 concatenate.7
  194.5 0.0 all-gather.2.cloned.1.call-update
  194.5 115.3 %all-gather.2.cloned.1.call-done = bf16[256,129,128]{2,1,0:T(8,128)(2,1)} async-done(((bf16[1,129,128]{2,1,0:T(8,128)(2,1)}), bf16[256,129,128]{2,1,0:T(8,128)(2,1)}) %all-gather.2.cloned.1.call-update) | async-done | bytes 8454160 | tf_op jit(solution)/shard_map/all_gather | solution.py:111
  309.8 13.5 %reshape.81 = bf16[8,32,16512]{2,1,0:T(8,128)(2,1)} reshape(bf16[256,129,128]{2,1,0:T(8,128)(2,1)} %all-gather.2.cloned.1.call-done) | data formatting | bytes 16908288 | tf_op jit(solution)/shard_map/reshape | solution.py:112
  323.3 0.0 copy-done.6
  323.3 0.0 copy-done.7
  323.3 0.0 copy-done.3
  323.3 0.0 copy-done.4
  323.4 0.0 copy-start
  323.4 1.1 slice.33
  324.4 6.0 %slice.32 = bf16[8,32,8192]{2,1,0:T(8,128)(2,1)} slice(bf16[8,32,16512]{2,1,0:T(8,128)(2,1)} %reshape.81), slice={[0:8], [0:32], [8256:16448]} | slice | bytes 8388608 | tf_op jit(solution)/shard_map/slice | solution.py:120
  330.4 2.3 slice.31
  332.8 0.7 reshape.86
  333.5 3.4 copy.36
  336.9 1.0 bitcast_bitcast_fusion
  337.9 2.7 copy.33
  340.6 6.2 %copy.41 = bf16[64,8,32,128]{3,1,2,0:T(8,128)(2,1)} copy(bf16[64,8,32,128]{3,2,1,0:T(8,128)(2,1)S(1)} %bitcast.43) | data formatting | bytes 8388608
  346.8 9.7 %reshape.82 = bf16[8,32,24,344]{3,2,1,0:T(8,128)(2,1)} reshape(bf16[8,32,8256]{2,1,0:T(8,128)(2,1)} %slice.31) | data formatting | bytes 8454144 | tf_op jit(solution)/shard_map/reshape | solution.py:115
  356.5 5.3 %copy.32 = bf16[8,24,32,344]{3,2,1,0:T(8,128)(2,1)} copy(bf16[8,24,32,344]{3,1,2,0:T(8,128)(2,1)} %bitcast.40) | data formatting | bytes 8454144 | tf_op jit(solution)/shard_map/transpose | solution.py:116
  361.8 9.9 %reshape.83 = bf16[192,11008]{1,0:T(8,128)(2,1)} reshape(bf16[8,24,32,344]{3,2,1,0:T(8,128)(2,1)} %copy.32) | data formatting | bytes 8454144 | tf_op jit(solution)/shard_map/reshape | solution.py:117
  (7 shorter events, 0.0 us)
Async XLA Ops:
  7.2 5.6 %copy-start.1 = (f32[1,24,11008]{2,1,0:T(8,128)S(1)}, f32[1,24,11008]{2,1,0:T(8,128)}, u32[]{:S(2)}) copy-start(f32[1,24,11008]{2,1,0:T(8,128)} %param.12) | copy-start | bytes 3170308
  7.2 97.3 %reduce-scatter.4.cloned.1.call-start = ((), (), s32[]{:S(2)}) async-start(), calls=%async_computation.2 | async-start | bytes 2297856
  17.7 86.8 %copy-start.12 = (f32[16]{0:T(128)S(1)}, f32[16]{0:T(128)}, u32[]{:S(2)}) copy-start(f32[16]{0:T(128)} %param.17) | copy-start | bytes 196
  17.7 86.8 %copy-start.13 = (f32[16]{0:T(128)S(1)}, f32[16]{0:T(128)}, u32[]{:S(2)}) copy-start(f32[16]{0:T(128)} %param.20) | copy-start | bytes 196
  17.7 86.8 %copy-start.14 = (f32[16]{0:T(128)S(1)}, f32[16]{0:T(128)}, u32[]{:S(2)}) copy-start(f32[16]{0:T(128)} %param.23) | copy-start | bytes 196
  17.7 88.6 %copy-start.5 = (f32[64,128]{1,0:T(8,128)S(1)}, f32[64,128]{1,0:T(8,128)}, u32[]{:S(2)}) copy-start(f32[64,128]{1,0:T(8,128)} %param.16) | copy-start | bytes 98308
  17.7 88.6 %copy-start.10 = (f32[64,128]{1,0:T(8,128)S(1)}, f32[64,128]{1,0:T(8,128)}, u32[]{:S(2)}) copy-start(f32[64,128]{1,0:T(8,128)} %param.19) | copy-start | bytes 98308
  17.7 88.6 %copy-start.11 = (f32[64,128]{1,0:T(8,128)S(1)}, f32[64,128]{1,0:T(8,128)}, u32[]{:S(2)}) copy-start(f32[64,128]{1,0:T(8,128)} %param.22) | copy-start | bytes 98308
  17.7 91.1 %copy-start.2 = (f32[24,344]{1,0:T(8,128)S(1)}, f32[24,344]{1,0:T(8,128)}, u32[]{:S(2)}) copy-start(f32[24,344]{1,0:T(8,128)} %param.15) | copy-start | bytes 99076
  17.8 91.1 %copy-start.8 = (f32[24,344]{1,0:T(8,128)S(1)}, f32[24,344]{1,0:T(8,128)}, u32[]{:S(2)}) copy-start(f32[24,344]{1,0:T(8,128)} %param.21) | copy-start | bytes 99076
  17.8 91.1 %copy-start.9 = (f32[24,344]{1,0:T(8,128)S(1)}, f32[24,344]{1,0:T(8,128)}, u32[]{:S(2)}) copy-start(f32[24,344]{1,0:T(8,128)} %param.18) | copy-start | bytes 99076
  19.3 290.4 %all-gather.2.cloned.1.call-start = ((), (), s32[]{:S(2)}) async-start(), calls=%async_computation.1 | async-start | bytes 8947712 | tf_op jit(solution)/shard_map/all_gather | solution.py:111
  107.8 215.5 %copy-start.6 = (f32[64,128]{1,0:T(8,128)}, f32[64,128]{1,0:T(8,128)S(1)}, u32[]{:S(2)}) copy-start(f32[64,128]{1,0:T(8,128)S(1)} %get-tuple-element.32) | copy-start | bytes 98308
  107.8 215.5 %copy-start.7 = (f32[64,128]{1,0:T(8,128)}, f32[64,128]{1,0:T(8,128)S(1)}, u32[]{:S(2)}) copy-start(f32[64,128]{1,0:T(8,128)S(1)} %get-tuple-element.33) | copy-start | bytes 98308
  109.5 213.8 %copy-start.3 = (f32[24,344]{1,0:T(8,128)}, f32[24,344]{1,0:T(8,128)S(1)}, u32[]{:S(2)}) copy-start(f32[24,344]{1,0:T(8,128)S(1)} %get-tuple-element.34) | copy-start | bytes 99076
  109.5 213.8 %copy-start.4 = (f32[24,344]{1,0:T(8,128)}, f32[24,344]{1,0:T(8,128)S(1)}, u32[]{:S(2)}) copy-start(f32[24,344]{1,0:T(8,128)S(1)} %get-tuple-element.35) | copy-start | bytes 99076
  323.4 7.1 %copy-start = (bf16[8,32,16512]{2,1,0:T(8,128)(2,1)S(1)}, bf16[8,32,16512]{2,1,0:T(8,128)(2,1)}, u32[]{:S(2)}) copy-start(bf16[8,32,16512]{2,1,0:T(8,128)(2,1)} %reshape.81) | copy-start | bytes 25362436
Sparse Core Ops, SparseCore 0:
  19.5 84.9 reduce-scatter.3
  194.6 115.1 all-gather.1
where the time goes:
time: 380 us; the launch traced here: 378 us
  waiting for transfers between devices  200 us (53%)
  blocking collectives  78 us (21%)
  local copies, waits for them, and re-layouts  74.3 us (20%)
  between operations  18.5 us (5%)
  other arithmetic  7.16 us (2%)
    all_gather x1, waiting for transfers between devices, body(): whole = lax.all_gather(low, ('narrow', 'wide'), axis=0, tiled=True)  115 us
    unnamed x3, waiting for transfers between devices  85.1 us
    psum x1, blocking collectives, body(): lax.psum((weight_sums, (jnp.sum(up_update * up_update), jnp.sum(down_upda...  78 us
    reshape x2, local copies, waits for them, and re-layouts, body(): up_weights = whole[:, :, :up_size].reshape(n_narrow, n_wide, up_rows, up_...  19.5 us
    reshape x1, local copies, waits for them, and re-layouts, body(): whole = whole.reshape(n_narrow, n_wide, width)  13.5 us
    unnamed x35, local copies, waits for them, and re-layouts  13.1 us
  transfers between devices with their start and end apart: 2, of which 2 were waited for; matrix products, arithmetic and copies ran while one was open for 0% of the time, Pallas kernels for 0%

commit v1 on v0

--- a/solution.py
+++ b/solution.py
@@ -108,7 +108,12 @@
             jnp.zeros((width - total,), jnp.bfloat16),
         ]
     ).reshape(1, width // LANES, LANES)
-    whole = lax.all_gather(low, ("narrow", "wide"), axis=0, tiled=True)
+    whole = jnp.concatenate(
+        lax.all_to_all(
+            jnp.stack([low] * lax.axis_size(("narrow", "wide"))), ("narrow", "wide"), 0, 0
+        ),
+        axis=0,
+    )
     whole = whole.reshape(n_narrow, n_wide, width)
     up_weights = (
         whole[:, :, :up_size]

time: 380 us -> 472 us (1.24)
  blocking collectives: 78 us -> 285 us
  waiting for transfers between devices: 200 us -> 85.1 us
    all_to_all x0 -> x1, blocking collectives: none -> 207 us  [body(): lax.all_to_all(jnp.stack([low] * lax.axis_size(('narrow', 'wide'))), ('na...]
    all_gather x1 -> x0, waiting for transfers between devices: 115 us -> none  [body(): whole = lax.all_gather(low, ('narrow', 'wide'), axis=0, tiled=True)]
    another operation x0 -> x2, local copies, waits for them, and re-layouts: none -> 14.7 us  [the longest x1 13.5 us: body(): whole = whole.reshape(n_narrow, n_wide, width)]
    reshape x1 -> x0, local copies, waits for them, and re-layouts: 13.5 us -> none  [body(): whole = whole.reshape(n_narrow, n_wide, width)]
    unnamed x3 -> x2, waiting for transfers between devices: 85.1 us -> 85.1 us
  transfers between devices with their start and end apart: 2 -> 1, of which waited for: 2 -> 1; matrix products, arithmetic and copies ran while one was open for 0% -> 0% of each run, Pallas kernels for 0% -> 0%
where the time goes in v1:
time: 472 us; the launch traced here: 471 us
  blocking collectives  285 us (60%)
  waiting for transfers between devices  85.1 us (18%)
  local copies, waits for them, and re-layouts  74.8 us (16%)
  between operations  18.5 us (4%)
  other arithmetic  7.15 us (2%)
    all_to_all x1, blocking collectives, body(): lax.all_to_all(jnp.stack([low] * lax.axis_size(('narrow', 'wide'))), ('na...  207 us
    unnamed x2, waiting for transfers between devices  85.1 us
    psum x1, blocking collectives, body(): lax.psum((weight_sums, (jnp.sum(up_update * up_update), jnp.sum(down_upda...  78 us
    reshape x2, local copies, waits for them, and re-layouts, body(): up_weights = whole[:, :, :up_size].reshape(n_narrow, n_wide, up_rows, up_...  19.5 us
    another operation x1, local copies, waits for them, and re-layouts, body(): whole = whole.reshape(n_narrow, n_wide, width)  13.5 us
    unnamed x35, local copies, waits for them, and re-layouts  13.1 us
  transfers between devices with their start and end apart: 1, of which 1 were waited for; matrix products, arithmetic and copies ran while one was open for 0% of the time, Pallas kernels for 0%

profile of v1, /device:TPU:1, one launch (start us, length us, event | category | flops | bytes accessed | tf_op | source)
XLA Modules:
  0.0 470.9 jit_solution(5889122398310783000)
XLA Ops:
  7.2 0.0 copy-start.1
  7.2 0.0 reduce-scatter.4.cloned.1.call-start
  7.2 0.5 broadcast.51
  7.7 1.3 reduce.3
  9.1 0.1 reshape.72
  9.2 1.4 copy.34
  10.6 0.6 copy.31
  11.2 1.6 copy.43
  12.8 0.0 copy-done.1
  12.8 1.3 reshape_squeeze.6
  14.1 0.7 copy.42
  14.8 0.3 reshape.70
  15.1 2.5 concatenate.6
  17.7 0.0 copy-start.12
  17.7 0.0 copy-start.13
  17.7 0.0 copy-start.14
  17.7 0.0 copy-start.5
  17.7 0.0 copy-start.10
  17.7 0.0 copy-start.11
  17.7 0.0 copy-start.2
  17.8 0.0 copy-start.8
  17.8 0.0 copy-start.9
  17.8 1.5 reshape.73
  19.3 0.0 reduce-scatter.4.cloned.1.call-update
  19.3 85.1 %reduce-scatter.4.cloned.1.call-done = f32[1,129,128]{2,1,0:T(8,128)} async-done(((f32[32,129,128]{2,1,0:T(8,128)}), f32[1,129,128]{2,1,0:T(8,128)}) %reduce-scatter.4.cloned.1.call-update) | async-done | bytes 66064
  104.5 0.0 copy-done.12
  104.5 0.0 copy-done.13
  104.5 0.0 copy-done.14
  104.5 1.9 multiply_reduce_fusion.4
  106.3 0.0 copy-done.5
  106.3 0.0 copy-done.10
  106.3 0.0 copy-done.11
  106.3 1.5 multiply_reduce_fusion.2
  107.8 0.0 copy-start.6
  107.8 1.0 slice.21
  108.8 0.0 copy-done.2
  108.9 0.0 copy-done.8
  108.9 0.0 copy-done.9
  108.9 0.7 multiply_reduce_fusion
  109.5 78.0 %all-reduce.1 = (f32[]{:T(128)}, f32[]{:T(128)}, f32[]{:T(128)}, f32[]{:T(128)}, f32[]{:T(128)}, /*index=5*/f32[]{:T(128)}) all-reduce(f32[]{:T(128)} %get-tuple-element.13, f32[]{:T(128)} %get-tuple-element.12, f32[]{:T(128)} %get-tuple-element.15, f32[]{:T(128)} %get-tuple-element.14, ...), channel_id=1, replica_groups=mesh['wide'=32,'narrow'=8] {'wide','narrow'}, use_global_device_ids=true, to_apply=%region_2.0 | all-reduce | flops 6 | bytes 48 | tf_op jit(solution)/shard_map/psum | solution.py:89
  191.8 0.6 fusion.4
  192.5 0.1 reshape.74
  192.6 0.5 fusion.3
  193.1 0.6 convert_bitcast_fusion
  193.7 0.1 concatenate.7
  193.9 1.1 stack.3
  195.0 0.0 copy-done.6
  195.0 0.0 copy-done.7
  195.0 0.0 copy-done.3
  195.0 0.0 copy-done.4
  195.0 207.3 %all_to_all.5 = bf16[256,1,129,128]{3,2,1,0:T(8,128)(2,1)} all-to-all(bf16[256,1,129,128]{3,2,1,0:T(8,128)(2,1)S(1)} %stack.3), channel_id=1, replica_groups=mesh['wide'=32,'narrow'=8] {'narrow','wide'}, dimensions={0} | all-to-all | bytes 16908288 | tf_op jit(solution)/shard_map/all_to_all | solution.py:112
  402.3 13.5 %reshape_reshape.3 = bf16[8,32,16512]{2,1,0:T(8,128)(2,1)} reshape(bf16[256,1,129,128]{3,2,1,0:T(8,128)(2,1)} %all_to_all.5) | data formatting | bytes 16908288 | tf_op jit(solution)/shard_map/reshape;reshape | solution.py:117
  415.8 1.1 slice.33
  416.9 6.0 %slice.32 = bf16[8,32,8192]{2,1,0:T(8,128)(2,1)} slice(bf16[8,32,16512]{2,1,0:T(8,128)(2,1)} %reshape_reshape.3), slice={[0:8], [0:32], [8256:16448]} | slice | bytes 8388608 | tf_op jit(solution)/shard_map/slice | solution.py:125
  422.9 0.0 copy-done
  422.9 2.3 slice.31
  425.2 0.7 reshape.82
  425.9 3.4 copy.36
  429.3 1.0 bitcast_bitcast_fusion
  430.4 2.7 copy.33
  433.1 6.2 %copy.41 = bf16[64,8,32,128]{3,1,2,0:T(8,128)(2,1)} copy(bf16[64,8,32,128]{3,2,1,0:T(8,128)(2,1)S(1)} %bitcast.43) | data formatting | bytes 8388608
  439.2 9.7 %reshape.78 = bf16[8,32,24,344]{3,2,1,0:T(8,128)(2,1)} reshape(bf16[8,32,8256]{2,1,0:T(8,128)(2,1)} %slice.31) | data formatting | bytes 8454144 | tf_op jit(solution)/shard_map/reshape | solution.py:120
  448.9 5.3 %copy.32 = bf16[8,24,32,344]{3,2,1,0:T(8,128)(2,1)} copy(bf16[8,24,32,344]{3,1,2,0:T(8,128)(2,1)} %bitcast.40) | data formatting | bytes 8454144 | tf_op jit(solution)/shard_map/transpose | solution.py:121
  454.2 9.9 %reshape.79 = bf16[192,11008]{1,0:T(8,128)(2,1)} reshape(bf16[8,24,32,344]{3,2,1,0:T(8,128)(2,1)} %copy.32) | data formatting | bytes 8454144 | tf_op jit(solution)/shard_map/reshape | solution.py:122
  (6 shorter events, 0.0 us)
Async XLA Ops:
  7.2 5.6 %copy-start.1 = (f32[1,24,11008]{2,1,0:T(8,128)S(1)}, f32[1,24,11008]{2,1,0:T(8,128)}, u32[]{:S(2)}) copy-start(f32[1,24,11008]{2,1,0:T(8,128)} %param.12) | copy-start | bytes 3170308
  7.2 97.3 %reduce-scatter.4.cloned.1.call-start = ((), (), s32[]{:S(2)}) async-start(), calls=%async_computation.2 | async-start | bytes 2297856
  17.7 86.8 %copy-start.12 = (f32[16]{0:T(128)S(1)}, f32[16]{0:T(128)}, u32[]{:S(2)}) copy-start(f32[16]{0:T(128)} %param.17) | copy-start | bytes 196
  17.7 86.8 %copy-start.13 = (f32[16]{0:T(128)S(1)}, f32[16]{0:T(128)}, u32[]{:S(2)}) copy-start(f32[16]{0:T(128)} %param.20) | copy-start | bytes 196
  17.7 86.8 %copy-start.14 = (f32[16]{0:T(128)S(1)}, f32[16]{0:T(128)}, u32[]{:S(2)}) copy-start(f32[16]{0:T(128)} %param.23) | copy-start | bytes 196
  17.7 88.6 %copy-start.5 = (f32[64,128]{1,0:T(8,128)S(1)}, f32[64,128]{1,0:T(8,128)}, u32[]{:S(2)}) copy-start(f32[64,128]{1,0:T(8,128)} %param.16) | copy-start | bytes 98308
  17.7 88.6 %copy-start.10 = (f32[64,128]{1,0:T(8,128)S(1)}, f32[64,128]{1,0:T(8,128)}, u32[]{:S(2)}) copy-start(f32[64,128]{1,0:T(8,128)} %param.19) | copy-start | bytes 98308
  17.7 88.6 %copy-start.11 = (f32[64,128]{1,0:T(8,128)S(1)}, f32[64,128]{1,0:T(8,128)}, u32[]{:S(2)}) copy-start(f32[64,128]{1,0:T(8,128)} %param.22) | copy-start | bytes 98308
  17.7 91.1 %copy-start.2 = (f32[24,344]{1,0:T(8,128)S(1)}, f32[24,344]{1,0:T(8,128)}, u32[]{:S(2)}) copy-start(f32[24,344]{1,0:T(8,128)} %param.15) | copy-start | bytes 99076
  17.8 91.1 %copy-start.8 = (f32[24,344]{1,0:T(8,128)S(1)}, f32[24,344]{1,0:T(8,128)}, u32[]{:S(2)}) copy-start(f32[24,344]{1,0:T(8,128)} %param.21) | copy-start | bytes 99076
  17.8 91.1 %copy-start.9 = (f32[24,344]{1,0:T(8,128)S(1)}, f32[24,344]{1,0:T(8,128)}, u32[]{:S(2)}) copy-start(f32[24,344]{1,0:T(8,128)} %param.18) | copy-start | bytes 99076
  107.8 87.2 %copy-start.6 = (f32[64,128]{1,0:T(8,128)}, f32[64,128]{1,0:T(8,128)S(1)}, u32[]{:S(2)}) copy-start(f32[64,128]{1,0:T(8,128)S(1)} %get-tuple-element.32) | copy-start | bytes 98308
  107.8 87.2 %copy-start.7 = (f32[64,128]{1,0:T(8,128)}, f32[64,128]{1,0:T(8,128)S(1)}, u32[]{:S(2)}) copy-start(f32[64,128]{1,0:T(8,128)S(1)} %get-tuple-element.33) | copy-start | bytes 98308
  109.5 85.5 %copy-start.3 = (f32[24,344]{1,0:T(8,128)}, f32[24,344]{1,0:T(8,128)S(1)}, u32[]{:S(2)}) copy-start(f32[24,344]{1,0:T(8,128)S(1)} %get-tuple-element.34) | copy-start | bytes 99076
  109.5 85.5 %copy-start.4 = (f32[24,344]{1,0:T(8,128)}, f32[24,344]{1,0:T(8,128)S(1)}, u32[]{:S(2)}) copy-start(f32[24,344]{1,0:T(8,128)S(1)} %get-tuple-element.35) | copy-start | bytes 99076
  415.8 7.1 %copy-start = (bf16[8,32,16512]{2,1,0:T(8,128)(2,1)S(1)}, bf16[8,32,16512]{2,1,0:T(8,128)(2,1)}, u32[]{:S(2)}) copy-start(bf16[8,32,16512]{2,1,0:T(8,128)(2,1)} %reshape_reshape.3) | copy-start | bytes 25362436
Sparse Core Ops, SparseCore 0:
  19.5 84.9 reduce-scatter.3
